TPU v7x, 128 devices: a whole 4x4x4 slice. The times are simulated.
128 devices in a mesh: dp: 16 (over x, y_lo, core), tensor: 8 (over z, y_hi).
Axes of the slice: x: 4, y: 4 (y_hi: 2, y_lo: 2; y = y_hi * 2 + y_lo), z: 4, core: 2. Of those that a mesh axis runs over, the one named last changes fastest.
Arguments:
- rows_in: bfloat16 [2048, 6144], P('dp'), may hold values from -6 to 6
- out_grad: bfloat16 [2048, 6144], P('dp'), may hold values from -1.5 to 1.5
- gate_pre: bfloat16 [2048, 12288], P('dp', 'tensor'), may hold values from -5 to 5
- up_pre: bfloat16 [2048, 12288], P('dp', 'tensor'), may hold values from -5 to 5
- w_gate: bfloat16 [2, 6144, 12288], P(None, 'dp', 'tensor'), may hold values from -0.078125 to 0.078125
- w_up: bfloat16 [2, 6144, 12288], P(None, 'dp', 'tensor'), may hold values from -0.078125 to 0.078125
- w_down: bfloat16 [2, 12288, 6144], P(None, 'tensor', 'dp'), may hold values from -0.0546875 to 0.0546875
- live_rows: int32 [16], P('dp'), may hold values from 32 to 128, as said below
- block_expert: int32 [16], replicated, may hold values from 0 to 1, as said below
Outputs:
- input_grad: bfloat16 [2048, 6144], P('dp', 'tensor')
- grad_gate: bfloat16 [2, 6144, 12288], P(None, 'dp', 'tensor')
- grad_up: bfloat16 [2, 6144, 12288], P(None, 'dp', 'tensor')
- grad_down: bfloat16 [2, 12288, 6144], P(None, 'tensor', 'dp')
Inputs may be any that keep to these rules, and one draw needn't show every extreme that they name: `live_rows`: entry k counts the live rows among rank k's 128 rows; they come first and the rest are padding; some rank is full. `block_expert`: the expert of each aligned block of 128 rows; every expert owns at least one block.
All inputs are finite; a program needn't handle non-finite values.
Results may differ from a plain program's by a relative error of at most 0.005.
Values may be sent and summed in bfloat16 or wider, within the bound.
No kernel may reach another device: no remote copies, remote signals or barrier semaphores. Data moves between devices by JAX's collectives and lax.ppermute only.
A program may use at most 128 MiB of HBM per device.

v0:
```python
import numpy as np
import jax
import jax.numpy as jnp
from jax import lax
from jax.sharding import Mesh
from jax.sharding import PartitionSpec as P

BLOCK = 128
AXES = ("x", "ylo", "core", "z", "yhi")
SIZES = (4, 2, 2, 4, 2)
DP = ("x", "ylo", "core")
TP = ("z", "yhi")
CHIPS = ("x", "ylo")
N_DP = 16
N_TP = 8


def rank_of_pos(pos):
    core, x, ylo = (pos // 8, pos % 8 // 2, pos % 2)
    return x * 4 + ylo * 2 + core


POS_RANK = np.array([rank_of_pos(p) for p in range(N_DP)], np.int32)


def deliver_perm(k):
    pairs = []
    for i in range(N_DP):
        for t in range(N_TP):
            dest = rank_of_pos(2 * t + (i % 2 ^ k))
            pairs.append((i * N_TP + t, dest * N_TP + i // 2))
    return pairs


def contract_rows(left_op, right_op):
    return lax.dot_general(
        left_op, right_op, (((0,), (0,)), ((), ())), preferred_element_type=jnp.float32
    )


def contract_cols(left_op, right_op):
    return lax.dot_general(
        left_op, right_op, (((1,), (1,)), ((), ())), preferred_element_type=jnp.float32
    )


def expert_masks(block_expert, row_count, expert_count):
    spread = jnp.broadcast_to(block_expert[:, None], (row_count // BLOCK, BLOCK)).reshape(
        row_count, 1
    )
    return [(spread == which).astype(jnp.bfloat16) for which in range(expert_count)]


def to_gathered_order(cols):
    width = cols.shape[1]
    return cols.reshape(4, 2, 2, BLOCK, width).transpose(2, 0, 1, 3, 4).reshape(-1, width)


def shards(rows_in, out_grad, gate_pre, up_pre, w_gate, w_up, w_down, live_rows, block_expert):
    rows_dev = rows_in.shape[0]
    expert_count = w_gate.shape[0]
    ff = gate_pre.shape[1]
    dy_cols = to_gathered_order(
        lax.all_to_all(out_grad, DP, split_axis=1, concat_axis=0, tiled=True)
    )
    x_cols = to_gathered_order(lax.all_to_all(rows_in, DP, split_axis=1, concat_axis=0, tiled=True))
    row_count = dy_cols.shape[0]
    expert_g = jnp.take(block_expert, jnp.asarray(POS_RANK), axis=0)
    masks = expert_masks(expert_g, row_count, expert_count)
    positions = jnp.arange(rows_dev, dtype=jnp.int32)[:, None]
    row_mask = (positions < live_rows[0]).astype(jnp.float32)
    gate_vals = gate_pre.astype(jnp.float32)
    up_vals = up_pre.astype(jnp.float32)
    sigmoid = jax.nn.sigmoid(gate_vals)
    silu_vals = gate_vals * sigmoid
    hidden = (silu_vals * up_vals * row_mask).astype(jnp.bfloat16)
    result = jnp.zeros((row_count, ff), jnp.float32)
    for which in range(expert_count):
        result = result + contract_cols(dy_cols * masks[which], w_down[which])
    result = lax.psum_scatter(
        result.reshape(2, row_count // 2, ff), "core", scatter_dimension=0, tiled=True
    ).reshape(row_count // 2, ff)
    hidden_grad = lax.psum_scatter(result, CHIPS, scatter_dimension=0, tiled=True)
    up_grad = (hidden_grad * silu_vals * row_mask).astype(jnp.bfloat16)
    gate_grad = (
        hidden_grad * up_vals * sigmoid * (1.0 + gate_vals * (1.0 - sigmoid)) * row_mask
    ).astype(jnp.bfloat16)
    packed = jnp.stack([hidden, gate_grad, up_grad], axis=1)
    packed = lax.all_gather(packed, CHIPS, axis=0, tiled=True)
    packed = lax.all_gather(packed, "core", axis=0, tiled=True)
    hid_g, gate_g, up_g = (packed[:, 0], packed[:, 1], packed[:, 2])
    down_terms = []
    gate_terms = []
    up_terms = []
    partial_rows = jnp.zeros((row_count, w_gate.shape[1]), jnp.float32)
    for which in range(expert_count):
        down_terms.append(contract_rows(hid_g * masks[which], dy_cols))
        gate_masked = gate_g * masks[which]
        up_masked = up_g * masks[which]
        gate_terms.append(contract_rows(x_cols, gate_masked))
        up_terms.append(contract_rows(x_cols, up_masked))
        partial_rows = (
            partial_rows
            + contract_cols(gate_masked, w_gate[which])
            + contract_cols(up_masked, w_up[which])
        )
    down_total = jnp.stack(down_terms, 0)
    gate_total = jnp.stack(gate_terms, 0)
    up_total = jnp.stack(up_terms, 0)
    width = partial_rows.shape[1]
    summed = lax.psum_scatter(
        partial_rows.reshape(N_TP, row_count // N_TP, width), TP, scatter_dimension=0, tiled=True
    ).reshape(2, rows_dev, width)
    core = lax.axis_index("core")
    ylo = lax.axis_index("ylo")
    got = []
    for k in range(2):
        piece = lax.dynamic_index_in_dim(summed, core ^ k, 0, keepdims=False)
        got.append(lax.ppermute(piece, AXES, deliver_perm(k)))
    first = jnp.where(ylo == 0, got[0], got[1])
    second = jnp.where(ylo == 0, got[1], got[0])
    input_grad = jnp.concatenate([first, second], axis=1).astype(jnp.bfloat16)
    return (
        input_grad,
        gate_total.astype(jnp.bfloat16),
        up_total.astype(jnp.bfloat16),
        down_total.astype(jnp.bfloat16),
    )


def solution(mesh):
    fine = Mesh(mesh.devices.reshape(SIZES), AXES)
    return jax.shard_map(
        shards,
        mesh=fine,
        in_specs=(
            P(DP, None),
            P(DP, None),
            P(DP, TP),
            P(DP, TP),
            P(None, DP, TP),
            P(None, DP, TP),
            P(None, TP, DP),
            P(DP),
            P(),
        ),
        out_specs=(P(DP, TP), P(None, DP, TP), P(None, DP, TP), P(None, TP, DP)),
        check_vma=False,
    )
```

profile of v0, /device:TPU:57, one launch (start us, length us, event | category | flops | bytes accessed | tf_op | source)
XLA Modules:
  0.0 575.7 jit_solution(3465949403237092074)
XLA Ops:
  7.2 2.6 copy.28
  9.8 6.2 %all-to-all-start = ((bf16[128,16,384]{0,2,1:T(8,128)(2,1)}), bf16[128,16,384]{0,2,1:T(8,128)(2,1)S(1)}, u32[]{:S(2)}, u32[]{:S(2)}) async-start(bf16[128,16,384]{0,2,1:T(8,128)(2,1)} %bitcast.2), calls=%async_computation | async-start | bytes 3145728 | tf_op jit(solution)/shard_map/all_to_all | solution.py:64
  16.1 0.7 gather_fusion
  17.2 20.2 %all-to-all-done = bf16[128,16,384]{0,2,1:T(8,128)(2,1)S(1)} async-done(((bf16[128,16,384]{0,2,1:T(8,128)(2,1)}), bf16[128,16,384]{0,2,1:T(8,128)(2,1)S(1)}, u32[]{:S(2)}, u32[]{:S(2)}) %all-to-all-start) | async-done | bytes 1572896 | tf_op jit(solution)/shard_map/all_to_all | solution.py:64
  37.4 0.9 copy.29
  38.2 0.4 broadcast_multiply_fusion
  38.6 0.2 copy.31
  38.8 0.2 copy.33
  39.0 1.4 copy-done.2
  40.5 3.5 fusion.77
  43.9 6.5 %convolution_add_fusion = f32[2048,1536]{1,0:T(8,128)} fusion(f32[2048,1536]{1,0:T(8,128)S(1)} %fusion.77, bf16[2048,384]{1,0:T(8,128)(2,1)S(1)} %bitcast.138, bf16[2,1536,384]{2,1,0:T(8,128)(2,1)S(1)} %copy-done.2), kind=kOutput, calls=%fused_computation.1 | convolution fusion | flops 2419064832 | bytes 27918336 | tf_op jit(solution)/shard_map/dot_general | solution.py:42
  50.6 25.1 %reduce-scatter.4.cloned.1.call-done = f32[1,1024,1536]{2,1,0:T(8,128)} async-done(((f32[2,1024,1536]{2,1,0:T(8,128)}), f32[1,1024,1536]{2,1,0:T(8,128)}) %reduce-scatter.4.cloned.1.call-update) | async-done | bytes 6291472 | tf_op jit(solution)/shard_map/reduce_scatter | solution.py:80
  76.4 131.5 %reduce-scatter.6.cloned.1.call-done = f32[128,1536]{1,0:T(8,128)} async-done(((f32[1024,1536]{1,0:T(8,128)}), f32[128,1536]{1,0:T(8,128)}) %reduce-scatter.6.cloned.1.call-update) | async-done | bytes 786448 | tf_op jit(solution)/shard_map/reduce_scatter | solution.py:83
  208.0 1.7 fusion.97
  209.7 1.1 pad_maximum_fusion.3
  210.9 189.0 %all-gather.3.cloned.1.call-done = bf16[1024,3,1536]{2,0,1:T(8,128)(2,1)} async-done(((bf16[128,3,1536]{2,0,1:T(8,128)(2,1)}), bf16[1024,3,1536]{2,0,1:T(8,128)(2,1)}) %all-gather.3.cloned.1.call-update) | async-done | bytes 9437200 | tf_op jit(solution)/shard_map/all_gather | solution.py:89
  399.9 1.4 copy-done.3
  401.3 1.6 copy.34
  402.9 7.1 %all-to-all-start.1 = ((bf16[128,16,384]{0,2,1:T(8,128)(2,1)}), bf16[128,16,384]{0,2,1:T(8,128)(2,1)S(1)}, u32[]{:S(2)}, u32[]{:S(2)}) async-start(bf16[128,16,384]{0,2,1:T(8,128)(2,1)} %bitcast.142), calls=%async_computation.4 | async-start | bytes 3145728 | tf_op jit(solution)/shard_map/all_to_all | solution.py:66
  410.0 0.5 reduce-scatter.8.cloned.1.call-start
  410.6 28.3 %all-gather.5.cloned.1.call-done = bf16[2048,3,1536]{2,0,1:T(8,128)(2,1)} async-done(((bf16[1024,3,1536]{2,0,1:T(8,128)(2,1)}), bf16[2048,3,1536]{2,0,1:T(8,128)(2,1)}) %all-gather.5.cloned.1.call-update) | async-done | bytes 18874384 | tf_op jit(solution)/shard_map/all_gather | solution.py:90
  438.9 8.3 %fusion.6 = f32[2048,384]{1,0:T(8,128)} fusion(bf16[2048,3,1536]{2,0,1:T(8,128)(2,1)} %all-gather.5.cloned.1.call-done, bf16[2048]{0:T(1024)(128)(2,1)S(1)} %get-tuple-element.31, bf16[2,384,1536]{2,1,0:T(8,128)(2,1)} %param.15), kind=kOutput, calls=%fused_computation.8 | convolution fusion | flops 2419064832 | bytes 10620928 | tf_op jit(solution)/shard_map/dot_general | solution.py:42
  447.3 1.3 copy-done.10
  448.6 0.7 copy-done.11
  449.2 5.2 fusion.14
  454.4 5.2 fusion.18
  459.6 7.3 %add_add_fusion = f32[2048,384]{1,0:T(8,128)} fusion(f32[2048,384]{1,0:T(8,128)} %fusion.6, f32[2048,384]{1,0:T(8,128)} %fusion.18, f32[2048,384]{1,0:T(8,128)} %fusion.14, bf16[2048,3,1536]{2,0,1:T(8,128)(2,1)S(1)} %copy-done.10, bf16[2048]{0:T(1024)(128)(2,1)S(1)} %get-tuple-element.31, bf16[2,384,1536]{2,1,0:T(8,128)(2,1)S(1)} %copy-done.12), kind=kOutput, calls=%fused_computation.30 | convolution fusion | flops 2421424128 | bytes 20058112 | tf_op jit(solution)/shard_map/dot_general | solution.py:42
  466.9 1.6 copy.36
  468.5 1.7 copy.37
  470.2 6.5 %fusion.63 = bf16[1,384,1536]{1,2,0:T(8,128)(2,1)S(1)} fusion(bf16[2048,384]{1,0:T(8,128)(2,1)S(1)} %bitcast.147, bf16[2048,3,1536]{2,0,1:T(8,128)(2,1)} %all-gather.5.cloned.1.call-done, bf16[2048]{0:T(1024)(128)(2,1)S(1)} %get-tuple-element.31), kind=kOutput, calls=%fused_computation.50 | convolution fusion | flops 2419654656 | bytes 9048064 | tf_op jit(solution)/shard_map/dot_general | solution.py:36
  476.8 6.7 %fusion.69 = bf16[1,384,1536]{1,2,0:T(8,128)(2,1)S(1)} fusion(bf16[2048,384]{1,0:T(8,128)(2,1)S(1)} %bitcast.148, bf16[2048,3,1536]{2,0,1:T(8,128)(2,1)} %all-gather.5.cloned.1.call-done, bf16[2048]{0:T(1024)(128)(2,1)S(1)} %get-tuple-element.32), kind=kOutput, calls=%fused_computation.52 | convolution fusion | flops 2419654656 | bytes 9048064 | tf_op jit(solution)/shard_map/dot_general | solution.py:36
  483.5 0.3 pad_maximum_fusion
  483.9 1.1 copy-done.6
  485.0 3.7 fusion.60
  488.6 3.9 fusion.66
  492.6 1.7 pad_maximum_fusion.1
  494.2 0.2 copy-done.4
  494.4 3.7 fusion.54
  498.1 4.7 fusion.57
  502.8 41.4 %reduce-scatter.8.cloned.1.call-done = f32[1,256,384]{2,1,0:T(8,128)} async-done(((f32[8,256,384]{2,1,0:T(8,128)}), f32[1,256,384]{2,1,0:T(8,128)}) %reduce-scatter.8.cloned.1.call-update) | async-done | bytes 393232 | tf_op jit(solution)/shard_map/reduce_scatter | solution.py:111
  544.2 1.7 dynamic-slice_bitcast_fusion.1
  545.9 6.2 %collective-permute-start = (bf16[128,384]{1,0:T(8,128)(2,1)}, bf16[128,384]{1,0:T(8,128)(2,1)}, u32[]{:S(2)}, u32[]{:S(2)}) collective-permute-start(bf16[128,384]{1,0:T(8,128)(2,1)} %get-tuple-element.25), channel_id=1, source_target_pairs={{0,0},{1,32},{2,64},{3,96},{4,8},{5,40},{6,72},{7,104},{8,16},{9,4... | collective-permute-start | bytes 294920 | tf_op jit(solution)/shard_map/ppermute | solution.py:119
  552.1 5.3 collective-permute-start.1
  557.4 2.9 pad_maximum_fusion.2
  560.4 2.6 copy.38
  563.0 4.3 copy.39
  567.2 1.0 select_convert_fusion.1
  568.2 0.7 pad_maximum_fusion.4
  (51 shorter events, 0.8 us)
Async XLA Ops:
  7.2 8.9 %copy-start = (s32[16]{0:T(128)S(1)}, s32[16]{0:T(128)}, u32[]{:S(2)}) copy-start(s32[16]{0:T(128)} %param.18) | copy-start | bytes 196
  9.8 6.3 %copy-start.9 = (s32[16]{0:T(128)S(1)}, s32[16]{0:T(128)}, u32[]{:S(2)}) copy-start(s32[16]{0:T(128)} %constant.52) | copy-start | bytes 196
  9.8 27.6 %all-to-all-start = ((bf16[128,16,384]{0,2,1:T(8,128)(2,1)}), bf16[128,16,384]{0,2,1:T(8,128)(2,1)S(1)}, u32[]{:S(2)}, u32[]{:S(2)}) async-start(bf16[128,16,384]{0,2,1:T(8,128)(2,1)} %bitcast.2), calls=%async_computation | async-start | bytes 3145728 | tf_op jit(solution)/shard_map/all_to_all | solution.py:64
  16.0 59.6 %reduce-scatter.4.cloned.1.call-start = ((), (), s32[]{:S(2)}) async-start(), calls=%async_computation.5 | async-start | bytes 18874368 | tf_op jit(solution)/shard_map/reduce_scatter | solution.py:80
  38.8 1.7 copy-start.2
  50.5 157.4 %reduce-scatter.6.cloned.1.call-start = ((), (), s32[]{:S(2)}) async-start(), calls=%async_computation.6 | async-start | bytes 7077888 | tf_op jit(solution)/shard_map/reduce_scatter | solution.py:83
  75.6 132.3 %copy-start.7 = (bf16[128,1536]{1,0:T(8,128)(2,1)S(1)}, bf16[128,1536]{1,0:T(8,128)(2,1)}, u32[]{:S(2)}) copy-start(bf16[128,1536]{1,0:T(8,128)(2,1)} %param.12) | copy-start | bytes 1179652
  75.6 132.3 %copy-start.8 = (bf16[128,1536]{1,0:T(8,128)(2,1)S(1)}, bf16[128,1536]{1,0:T(8,128)(2,1)}, u32[]{:S(2)}) copy-start(bf16[128,1536]{1,0:T(8,128)(2,1)} %param.13) | copy-start | bytes 1179652
  75.7 324.2 %all-gather.3.cloned.1.call-start = ((), (), s32[]{:S(2)}) async-start(), calls=%async_computation.7 | async-start | bytes 10616832 | tf_op jit(solution)/shard_map/all_gather | solution.py:89
  210.8 228.1 %all-gather.5.cloned.1.call-start = ((), (), s32[]{:S(2)}) async-start(), calls=%async_computation.8 | async-start | bytes 28311552 | tf_op jit(solution)/shard_map/all_gather | solution.py:90
  399.9 1.4 copy-start.3
  402.9 64.0 %all-to-all-start.1 = ((bf16[128,16,384]{0,2,1:T(8,128)(2,1)}), bf16[128,16,384]{0,2,1:T(8,128)(2,1)S(1)}, u32[]{:S(2)}, u32[]{:S(2)}) async-start(bf16[128,16,384]{0,2,1:T(8,128)(2,1)} %bitcast.142), calls=%async_computation.4 | async-start | bytes 3145728 | tf_op jit(solution)/shard_map/all_to_all | solution.py:66
  410.0 134.2 %reduce-scatter.8.cloned.1.call-start = ((), (), s32[]{:S(2)}) async-start(), calls=%async_computation.9 | async-start | bytes 3538944 | tf_op jit(solution)/shard_map/reduce_scatter | solution.py:111
  438.9 9.7 %copy-start.10 = (bf16[2048,3,1536]{2,0,1:T(8,128)(2,1)S(1)}, bf16[2048,3,1536]{2,0,1:T(8,128)(2,1)}, u32[]{:S(2)}) copy-start(bf16[2048,3,1536]{2,0,1:T(8,128)(2,1)} %all-gather.5.cloned.1.call-done) | copy-start | bytes 56623108
  438.9 10.3 %copy-start.11 = (bf16[2,384,1536]{2,1,0:T(8,128)(2,1)S(1)}, bf16[2,384,1536]{2,1,0:T(8,128)(2,1)}, u32[]{:S(2)}) copy-start(bf16[2,384,1536]{2,1,0:T(8,128)(2,1)} %param.15) | copy-start | bytes 7077892
  449.2 5.2 copy-start.12
  468.5 1.7 copy-start.5
  470.2 13.6 %slice-start = ((s8[18874368]{0:T(1024)(128)(4,1)}), s8[4194304]{0:T(1024)(128)(4,1)S(1)}, s32[]{:S(2)}) async-start(s8[18874368]{0:T(1024)(128)(4,1)} %bitcast.152), calls=%async_computation.10 | async-start | bytes 8388608
  470.2 13.6 %slice-start.1 = ((s8[18874368]{0:T(1024)(128)(4,1)}), s8[4194304]{0:T(1024)(128)(4,1)S(1)}, s32[]{:S(2)}) async-start(s8[18874368]{0:T(1024)(128)(4,1)} %bitcast.152), calls=%async_computation.11 | async-start | bytes 8388608
  470.2 13.6 %slice-start.2 = ((s8[18874368]{0:T(1024)(128)(4,1)}), s8[4194304]{0:T(1024)(128)(4,1)S(1)}, s32[]{:S(2)}) async-start(s8[18874368]{0:T(1024)(128)(4,1)} %bitcast.152), calls=%async_computation.12 | async-start | bytes 8388608
  476.8 7.1 %slice-start.3 = ((s8[18874368]{0:T(1024)(128)(4,1)}), s8[4194304]{0:T(1024)(128)(4,1)S(1)}, s32[]{:S(2)}) async-start(s8[18874368]{0:T(1024)(128)(4,1)} %bitcast.152), calls=%async_computation.13 | async-start | bytes 8388608
  476.8 7.1 %slice-start.4 = ((s8[18874368]{0:T(1024)(128)(4,1)}), s8[2097152]{0:T(1024)(128)(4,1)S(1)}, s32[]{:S(2)}) async-start(s8[18874368]{0:T(1024)(128)(4,1)} %bitcast.152), calls=%async_computation.14 | async-start | bytes 4194304
  483.5 1.4 copy-start.6
  492.5 1.9 copy-start.4
  545.9 21.3 %collective-permute-start = (bf16[128,384]{1,0:T(8,128)(2,1)}, bf16[128,384]{1,0:T(8,128)(2,1)}, u32[]{:S(2)}, u32[]{:S(2)}) collective-permute-start(bf16[128,384]{1,0:T(8,128)(2,1)} %get-tuple-element.25), channel_id=1, source_target_pairs={{0,0},{1,32},{2,64},{3,96},{4,8},{5,40},{6,72},{7,104},{8,16},{9,4... | collective-permute-start | bytes 294920 | tf_op jit(solution)/shard_map/ppermute | solution.py:119
  552.1 15.1 %collective-permute-start.1 = (bf16[128,384]{1,0:T(8,128)(2,1)}, bf16[128,384]{1,0:T(8,128)(2,1)}, u32[]{:S(2)}, u32[]{:S(2)}) collective-permute-start(bf16[128,384]{1,0:T(8,128)(2,1)} %get-tuple-element.26), channel_id=1, source_target_pairs={{0,16},{1,48},{2,80},{3,112},{4,24},{5,56},{6,88},{7,120},{8,0},{9... | collective-permute-start | bytes 294920 | tf_op jit(solution)/shard_map/ppermute | solution.py:119
  560.4 8.5 %copy-start.1 = (s32[16]{0:T(128)S(1)}, s32[16]{0:T(128)}, u32[]{:S(2)}) copy-start(s32[16]{0:T(128)} %param.18) | copy-start | bytes 196
Sparse Core Ops, SparseCore 0:
  50.6 24.9 reduce-scatter.3
  78.0 129.8 reduce-scatter.5
  210.9 188.9 all-gather.2
  401.4 37.4 all-gather.4
  467.0 77.1 reduce-scatter.7
where the time goes:
time: 582 us; the launch traced here: 576 us
  waiting for transfers between devices  436 us (75%)
  matrix products  65.2 us (11%)
  starting transfers between devices  25.5 us (4%)
  local copies, waits for them, and re-layouts  24.6 us (4%)
  between operations  15 us (3%)
  other arithmetic  9.76 us (2%)
    all_gather x1, waiting for transfers between devices, shards(): packed = lax.all_gather(packed, CHIPS, axis=0, tiled=True)  189 us
    reduce_scatter x1, waiting for transfers between devices, shards(): lax.psum_scatter(result, CHIPS, scatter_dimension=0, tiled=True)  132 us
    reduce_scatter x1, waiting for transfers between devices, shards(): lax.psum_scatter(partial_rows.reshape(N_TP, row_count // N_TP, width), TP...  41.4 us
    dot_general x6, matrix products, contract_cols(): lax.dot_general(left_op, right_op, (((1,), (1,)), ((), ())), preferred_el...  36 us
    dot_general x6, matrix products, contract_rows(): lax.dot_general(left_op, right_op, (((0,), (0,)), ((), ())), preferred_el...  29.2 us
    all_gather x1, waiting for transfers between devices, shards(): packed = lax.all_gather(packed, 'core', axis=0, tiled=True)  28.3 us
    reduce_scatter x1, waiting for transfers between devices, shards(): lax.psum_scatter(result.reshape(2, row_count // 2, ff), 'core', scatter_d...  25.1 us
    all_to_all x1, waiting for transfers between devices, shards(): lax.all_to_all(out_grad, DP, split_axis=1, concat_axis=0, tiled=True)  20.2 us
  transfers between devices with their start and end apart: 9, of which 6 were waited for; matrix products, arithmetic and copies ran while one was open for 13% of the time, Pallas kernels for 0%

commit v1 on v0

--- a/solution.py
+++ b/solution.py
@@ -86,7 +86,9 @@
         hidden_grad * up_vals * sigmoid * (1.0 + gate_vals * (1.0 - sigmoid)) * row_mask
     ).astype(jnp.bfloat16)
     packed = jnp.stack([hidden, gate_grad, up_grad], axis=1)
-    packed = lax.all_gather(packed, CHIPS, axis=0, tiled=True)
+    packed = jnp.concatenate(
+        lax.all_to_all(jnp.stack([packed] * lax.axis_size(CHIPS)), CHIPS, 0, 0), axis=0
+    )
     packed = lax.all_gather(packed, "core", axis=0, tiled=True)
     hid_g, gate_g, up_g = (packed[:, 0], packed[:, 1], packed[:, 2])
     down_terms = []

time: 582 us -> 510 us (0.88)
  waiting for transfers between devices: 436 us -> 246 us
  blocking collectives: 0 us -> 110 us
  local copies, waits for them, and re-layouts: 24.6 us -> 33.8 us
    all_gather x1 -> x0, waiting for transfers between devices: 189 us -> none  [shards(): packed = lax.all_gather(packed, CHIPS, axis=0, tiled=True)]
    all_to_all x0 -> x1, blocking collectives: none -> 110 us  [shards(): lax.all_to_all(jnp.stack([packed] * lax.axis_size(CHIPS)), CHIPS, 0, 0)]
    all_to_all x0 -> x1, local copies, waits for them, and re-layouts: none -> 8.25 us  [shards(): lax.all_to_all(jnp.stack([packed] * lax.axis_size(CHIPS)), CHIPS, 0, 0)]
  transfers between devices with their start and end apart: 9 -> 8, of which waited for: 6 -> 5; matrix products, arithmetic and copies ran while one was open for 13% -> 14% of each run, Pallas kernels for 0% -> 0%
where the time goes in v1:
time: 510 us; the launch traced here: 503 us
  waiting for transfers between devices  246 us (48%)
  blocking collectives  110 us (22%)
  matrix products  65.1 us (13%)
  local copies, waits for them, and re-layouts  33.8 us (7%)
  starting transfers between devices  23.8 us (5%)
  between operations  15 us (3%)
  other arithmetic  8.75 us (2%)
    reduce_scatter x1, waiting for transfers between devices, shards(): lax.psum_scatter(result, CHIPS, scatter_dimension=0, tiled=True)  132 us
    all_to_all x1, blocking collectives, shards(): lax.all_to_all(jnp.stack([packed] * lax.axis_size(CHIPS)), CHIPS, 0, 0)  110 us
    reduce_scatter x1, waiting for transfers between devices, shards(): lax.psum_scatter(partial_rows.reshape(N_TP, row_count // N_TP, width), TP...  41.8 us
    dot_general x6, matrix products, contract_cols(): lax.dot_general(left_op, right_op, (((1,), (1,)), ((), ())), preferred_el...  36.3 us
    dot_general x6, matrix products, contract_rows(): lax.dot_general(left_op, right_op, (((0,), (0,)), ((), ())), preferred_el...  28.8 us
    all_gather x1, waiting for transfers between devices, shards(): packed = lax.all_gather(packed, 'core', axis=0, tiled=True)  27.3 us
    reduce_scatter x1, waiting for transfers between devices, shards(): lax.psum_scatter(result.reshape(2, row_count // 2, ff), 'core', scatter_d...  25.1 us
    all_to_all x1, waiting for transfers between devices, shards(): lax.all_to_all(out_grad, DP, split_axis=1, concat_axis=0, tiled=True)  20.2 us
  transfers between devices with their start and end apart: 8, of which 5 were waited for; matrix products, arithmetic and copies ran while one was open for 14% of the time, Pallas kernels for 0%

profile of v1, /device:TPU:57, one launch (start us, length us, event | category | flops | bytes accessed | tf_op | source)
XLA Modules:
  0.0 502.8 jit_solution(12384394916500405793)
XLA Ops:
  7.2 2.6 copy.41
  9.8 6.2 %all-to-all-start = ((bf16[128,16,384]{0,2,1:T(8,128)(2,1)}), bf16[128,16,384]{0,2,1:T(8,128)(2,1)S(1)}, u32[]{:S(2)}, u32[]{:S(2)}) async-start(bf16[128,16,384]{0,2,1:T(8,128)(2,1)} %bitcast.2), calls=%async_computation | async-start | bytes 3145728 | tf_op jit(solution)/shard_map/all_to_all | solution.py:64
  16.1 0.7 gather_fusion
  17.2 20.2 %all-to-all-done = bf16[128,16,384]{0,2,1:T(8,128)(2,1)S(1)} async-done(((bf16[128,16,384]{0,2,1:T(8,128)(2,1)}), bf16[128,16,384]{0,2,1:T(8,128)(2,1)S(1)}, u32[]{:S(2)}, u32[]{:S(2)}) %all-to-all-start) | async-done | bytes 1572896 | tf_op jit(solution)/shard_map/all_to_all | solution.py:64
  37.4 0.9 copy.42
  38.2 0.4 broadcast_multiply_fusion
  38.6 0.2 copy.44
  39.0 1.5 copy-done.2
  40.5 3.5 fusion.77
  43.9 6.7 %convolution_add_fusion = f32[2048,1536]{1,0:T(8,128)} fusion(f32[2048,1536]{1,0:T(8,128)S(1)} %fusion.77, bf16[2048,384]{1,0:T(8,128)(2,1)S(1)} %bitcast.140, bf16[2,1536,384]{2,1,0:T(8,128)(2,1)S(1)} %copy-done.2), kind=kOutput, calls=%fused_computation.1 | convolution fusion | flops 2419064832 | bytes 27918336 | tf_op jit(solution)/shard_map/dot_general | solution.py:42
  50.7 25.1 %reduce-scatter.4.cloned.1.call-done = f32[1,1024,1536]{2,1,0:T(8,128)} async-done(((f32[2,1024,1536]{2,1,0:T(8,128)}), f32[1,1024,1536]{2,1,0:T(8,128)}) %reduce-scatter.4.cloned.1.call-update) | async-done | bytes 6291472 | tf_op jit(solution)/shard_map/reduce_scatter | solution.py:80
  76.6 131.5 %reduce-scatter.6.cloned.1.call-done = f32[128,1536]{1,0:T(8,128)} async-done(((f32[1024,1536]{1,0:T(8,128)}), f32[128,1536]{1,0:T(8,128)}) %reduce-scatter.6.cloned.1.call-update) | async-done | bytes 786448 | tf_op jit(solution)/shard_map/reduce_scatter | solution.py:83
  208.1 1.7 fusion.97
  209.9 1.0 stack.63
  211.0 110.4 %all_to_all.37 = bf16[8,128,3,1536]{3,1,2,0:T(8,128)(2,1)} all-to-all(bf16[8,128,3,1536]{3,1,2,0:T(8,128)(2,1)S(1)} %stack.63), channel_id=1, replica_groups=mesh['x'=4,'ylo'=2,'core'=2,'z'=4,'yhi'=2] {'x','ylo'}, dimensions={0} | all-to-all | bytes 18874368 | tf_op jit(solution)/shard_map/all_to_all | solution.py:90
  321.3 8.3 %copy.47 = bf16[8,128,3,1536]{3,1,0,2:T(8,128)(2,1)} copy(bf16[8,128,3,1536]{3,1,2,0:T(8,128)(2,1)} %all_to_all.37) | data formatting | bytes 18874368 | tf_op jit(solution)/shard_map/all_to_all | solution.py:90
  329.6 1.4 copy-done.3
  331.0 1.6 copy.48
  332.6 5.5 %all-to-all-start.2 = ((bf16[128,16,384]{0,2,1:T(8,128)(2,1)}), bf16[128,16,384]{0,2,1:T(8,128)(2,1)S(1)}, u32[]{:S(2)}, u32[]{:S(2)}) async-start(bf16[128,16,384]{0,2,1:T(8,128)(2,1)} %bitcast.144), calls=%async_computation.5 | async-start | bytes 3145728 | tf_op jit(solution)/shard_map/all_to_all | solution.py:66
  338.1 0.5 reduce-scatter.8.cloned.1.call-start
  338.7 27.3 %all-gather.2.cloned.1.call-done = bf16[2048,3,1536]{2,0,1:T(8,128)(2,1)} async-done(((bf16[1024,3,1536]{2,0,1:T(8,128)(2,1)}), bf16[2048,3,1536]{2,0,1:T(8,128)(2,1)}) %all-gather.2.cloned.1.call-update) | async-done | bytes 18874384 | tf_op jit(solution)/shard_map/all_gather | solution.py:92
  366.1 8.4 %fusion.14 = f32[2048,384]{1,0:T(8,128)} fusion(bf16[2048,3,1536]{2,0,1:T(8,128)(2,1)} %all-gather.2.cloned.1.call-done, bf16[2048]{0:T(1024)(128)(2,1)S(1)} %broadcast_bitcast_fusion.1, bf16[2,384,1536]{2,1,0:T(8,128)(2,1)} %param.15), kind=kOutput, calls=%fused_computation.16 | convolution fusion | flops 2419064832 | bytes 10620928 | tf_op jit(solution)/shard_map/dot_general | solution.py:42
  374.5 1.2 copy-done.10
  375.7 0.7 copy-done.12
  376.4 5.2 %fusion.18 = f32[2048,384]{1,0:T(8,128)} fusion(bf16[2048,3,1536]{2,0,1:T(8,128)(2,1)S(1)} %copy-done.10, bf16[2048]{0:T(1024)(128)(2,1)S(1)} %broadcast_bitcast_fusion.1, bf16[2,384,1536]{2,1,0:T(8,128)(2,1)S(1)} %copy-done.12), kind=kOutput, calls=%fused_computation.20 | convolution fusion | flops 2419064832 | bytes 10620928 | tf_op jit(solution)/shard_map/dot_general | solution.py:42
  381.6 5.2 %fusion.6 = f32[2048,384]{1,0:T(8,128)} fusion(bf16[2048,3,1536]{2,0,1:T(8,128)(2,1)S(1)} %copy-done.10, bf16[2048]{0:T(1024)(128)(2,1)S(1)} %broadcast_bitcast_fusion, bf16[2,384,1536]{2,1,0:T(8,128)(2,1)S(1)} %copy-done.11), kind=kOutput, calls=%fused_computation.8 | convolution fusion | flops 2419064832 | bytes 10620928 | tf_op jit(solution)/shard_map/dot_general | solution.py:42
  386.8 7.3 %add_add_fusion = f32[2048,384]{1,0:T(8,128)} fusion(f32[2048,384]{1,0:T(8,128)} %fusion.6, f32[2048,384]{1,0:T(8,128)} %fusion.18, f32[2048,384]{1,0:T(8,128)} %fusion.14, bf16[2048,3,1536]{2,0,1:T(8,128)(2,1)S(1)} %copy-done.10, bf16[2048]{0:T(1024)(128)(2,1)S(1)} %broadcast_bitcast_fusion, bf16[2,384,1536]{2,1,0:T(8,128)(2,1)S(1)} %copy-done.12), kind=kOutput, calls=%fused_computation.30 | convolution fusion | flops 2421424128 | bytes 20058112 | tf_op jit(solution)/shard_map/dot_general | solution.py:42
  394.1 1.6 copy.50
  395.7 1.7 copy.51
  397.5 6.5 %fusion.60 = bf16[1,384,1536]{1,2,0:T(8,128)(2,1)S(1)} fusion(bf16[2048,384]{1,0:T(8,128)(2,1)S(1)} %bitcast.149, bf16[2048,3,1536]{2,0,1:T(8,128)(2,1)} %all-gather.2.cloned.1.call-done, bf16[2048]{0:T(1024)(128)(2,1)S(1)} %broadcast_bitcast_fusion), kind=kOutput, calls=%fused_computation.49 | convolution fusion | flops 2419654656 | bytes 9048064 | tf_op jit(solution)/shard_map/dot_general | solution.py:36
  404.0 6.7 %fusion.66 = bf16[1,384,1536]{1,2,0:T(8,128)(2,1)S(1)} fusion(bf16[2048,384]{1,0:T(8,128)(2,1)S(1)} %bitcast.150, bf16[2048,3,1536]{2,0,1:T(8,128)(2,1)} %all-gather.2.cloned.1.call-done, bf16[2048]{0:T(1024)(128)(2,1)S(1)} %broadcast_bitcast_fusion.1), kind=kOutput, calls=%fused_computation.51 | convolution fusion | flops 2419654656 | bytes 9048064 | tf_op jit(solution)/shard_map/dot_general | solution.py:36
  410.7 0.3 pad_maximum_fusion.1
  411.1 1.1 copy-done.6
  412.2 3.6 fusion.63
  415.7 3.8 fusion.69
  419.6 1.7 pad_maximum_fusion
  421.2 0.2 copy-done.4
  421.4 3.6 fusion.54
  425.0 4.6 fusion.57
  429.6 41.8 %reduce-scatter.8.cloned.1.call-done = f32[1,256,384]{2,1,0:T(8,128)} async-done(((f32[8,256,384]{2,1,0:T(8,128)}), f32[1,256,384]{2,1,0:T(8,128)}) %reduce-scatter.8.cloned.1.call-update) | async-done | bytes 393232 | tf_op jit(solution)/shard_map/reduce_scatter | solution.py:113
  471.4 1.7 dynamic-slice_bitcast_fusion.1
  473.1 6.2 %collective-permute-start = (bf16[128,384]{1,0:T(8,128)(2,1)}, bf16[128,384]{1,0:T(8,128)(2,1)}, u32[]{:S(2)}, u32[]{:S(2)}) collective-permute-start(bf16[128,384]{1,0:T(8,128)(2,1)} %get-tuple-element.29), channel_id=1, source_target_pairs={{0,0},{1,32},{2,64},{3,96},{4,8},{5,40},{6,72},{7,104},{8,16},{9,4... | collective-permute-start | bytes 294920 | tf_op jit(solution)/shard_map/ppermute | solution.py:121
  479.4 5.2 %collective-permute-start.1 = (bf16[128,384]{1,0:T(8,128)(2,1)}, bf16[128,384]{1,0:T(8,128)(2,1)}, u32[]{:S(2)}, u32[]{:S(2)}) collective-permute-start(bf16[128,384]{1,0:T(8,128)(2,1)} %get-tuple-element.30), channel_id=1, source_target_pairs={{0,16},{1,48},{2,80},{3,112},{4,24},{5,56},{6,88},{7,120},{8,0},{9... | collective-permute-start | bytes 294920 | tf_op jit(solution)/shard_map/ppermute | solution.py:121
  484.6 2.9 pad_maximum_fusion.2
  487.5 2.6 copy.53
  490.1 4.3 copy.52
  494.4 1.0 select_convert_fusion.1
  495.4 0.7 pad_maximum_fusion.4
  (52 shorter events, 1.1 us)
Async XLA Ops:
  7.2 8.9 %copy-start = (s32[16]{0:T(128)S(1)}, s32[16]{0:T(128)}, u32[]{:S(2)}) copy-start(s32[16]{0:T(128)} %param.18) | copy-start | bytes 196
  9.8 6.3 %copy-start.9 = (s32[16]{0:T(128)S(1)}, s32[16]{0:T(128)}, u32[]{:S(2)}) copy-start(s32[16]{0:T(128)} %constant.52) | copy-start | bytes 196
  9.8 27.6 %all-to-all-start = ((bf16[128,16,384]{0,2,1:T(8,128)(2,1)}), bf16[128,16,384]{0,2,1:T(8,128)(2,1)S(1)}, u32[]{:S(2)}, u32[]{:S(2)}) async-start(bf16[128,16,384]{0,2,1:T(8,128)(2,1)} %bitcast.2), calls=%async_computation | async-start | bytes 3145728 | tf_op jit(solution)/shard_map/all_to_all | solution.py:64
  16.0 59.8 %reduce-scatter.4.cloned.1.call-start = ((), (), s32[]{:S(2)}) async-start(), calls=%async_computation.6 | async-start | bytes 18874368 | tf_op jit(solution)/shard_map/reduce_scatter | solution.py:80
  38.8 1.7 copy-start.2
  50.6 157.4 %reduce-scatter.6.cloned.1.call-start = ((), (), s32[]{:S(2)}) async-start(), calls=%async_computation.7 | async-start | bytes 7077888 | tf_op jit(solution)/shard_map/reduce_scatter | solution.py:83
  75.8 132.3 %copy-start.7 = (bf16[128,1536]{1,0:T(8,128)(2,1)S(1)}, bf16[128,1536]{1,0:T(8,128)(2,1)}, u32[]{:S(2)}) copy-start(bf16[128,1536]{1,0:T(8,128)(2,1)} %param.12) | copy-start | bytes 1179652
  75.8 132.3 %copy-start.8 = (bf16[128,1536]{1,0:T(8,128)(2,1)S(1)}, bf16[128,1536]{1,0:T(8,128)(2,1)}, u32[]{:S(2)}) copy-start(bf16[128,1536]{1,0:T(8,128)(2,1)} %param.13) | copy-start | bytes 1179652
  75.8 290.3 %all-gather.2.cloned.1.call-start = ((), (), s32[]{:S(2)}) async-start(), calls=%async_computation.8 | async-start | bytes 28311552 | tf_op jit(solution)/shard_map/all_gather | solution.py:92
  329.6 1.4 copy-start.3
  332.6 61.6 %all-to-all-start.2 = ((bf16[128,16,384]{0,2,1:T(8,128)(2,1)}), bf16[128,16,384]{0,2,1:T(8,128)(2,1)S(1)}, u32[]{:S(2)}, u32[]{:S(2)}) async-start(bf16[128,16,384]{0,2,1:T(8,128)(2,1)} %bitcast.144), calls=%async_computation.5 | async-start | bytes 3145728 | tf_op jit(solution)/shard_map/all_to_all | solution.py:66
  338.1 133.3 %reduce-scatter.8.cloned.1.call-start = ((), (), s32[]{:S(2)}) async-start(), calls=%async_computation.9 | async-start | bytes 3538944 | tf_op jit(solution)/shard_map/reduce_scatter | solution.py:113
  366.1 9.7 %copy-start.10 = (bf16[2048,3,1536]{2,0,1:T(8,128)(2,1)S(1)}, bf16[2048,3,1536]{2,0,1:T(8,128)(2,1)}, u32[]{:S(2)}) copy-start(bf16[2048,3,1536]{2,0,1:T(8,128)(2,1)} %all-gather.2.cloned.1.call-done) | copy-start | bytes 56623108
  366.1 10.3 %copy-start.12 = (bf16[2,384,1536]{2,1,0:T(8,128)(2,1)S(1)}, bf16[2,384,1536]{2,1,0:T(8,128)(2,1)}, u32[]{:S(2)}) copy-start(bf16[2,384,1536]{2,1,0:T(8,128)(2,1)} %param.14) | copy-start | bytes 7077892
  376.4 5.2 %copy-start.11 = (bf16[2,384,1536]{2,1,0:T(8,128)(2,1)S(1)}, bf16[2,384,1536]{2,1,0:T(8,128)(2,1)}, u32[]{:S(2)}) copy-start(bf16[2,384,1536]{2,1,0:T(8,128)(2,1)} %param.15) | copy-start | bytes 7077892
  395.7 1.7 copy-start.5
  397.4 13.6 %slice-start = ((s8[18874368]{0:T(1024)(128)(4,1)}), s8[4194304]{0:T(1024)(128)(4,1)S(1)}, s32[]{:S(2)}) async-start(s8[18874368]{0:T(1024)(128)(4,1)} %bitcast.154), calls=%async_computation.10 | async-start | bytes 8388608
  397.4 13.6 %slice-start.1 = ((s8[18874368]{0:T(1024)(128)(4,1)}), s8[4194304]{0:T(1024)(128)(4,1)S(1)}, s32[]{:S(2)}) async-start(s8[18874368]{0:T(1024)(128)(4,1)} %bitcast.154), calls=%async_computation.11 | async-start | bytes 8388608
  397.5 13.6 %slice-start.2 = ((s8[18874368]{0:T(1024)(128)(4,1)}), s8[4194304]{0:T(1024)(128)(4,1)S(1)}, s32[]{:S(2)}) async-start(s8[18874368]{0:T(1024)(128)(4,1)} %bitcast.154), calls=%async_computation.12 | async-start | bytes 8388608
  404.0 7.1 %slice-start.3 = ((s8[18874368]{0:T(1024)(128)(4,1)}), s8[4194304]{0:T(1024)(128)(4,1)S(1)}, s32[]{:S(2)}) async-start(s8[18874368]{0:T(1024)(128)(4,1)} %bitcast.154), calls=%async_computation.13 | async-start | bytes 8388608
  404.0 7.1 %slice-start.4 = ((s8[18874368]{0:T(1024)(128)(4,1)}), s8[2097152]{0:T(1024)(128)(4,1)S(1)}, s32[]{:S(2)}) async-start(s8[18874368]{0:T(1024)(128)(4,1)} %bitcast.154), calls=%async_computation.14 | async-start | bytes 4194304
  410.7 1.4 copy-start.6
  419.5 1.9 copy-start.4
  473.1 21.3 %collective-permute-start = (bf16[128,384]{1,0:T(8,128)(2,1)}, bf16[128,384]{1,0:T(8,128)(2,1)}, u32[]{:S(2)}, u32[]{:S(2)}) collective-permute-start(bf16[128,384]{1,0:T(8,128)(2,1)} %get-tuple-element.29), channel_id=1, source_target_pairs={{0,0},{1,32},{2,64},{3,96},{4,8},{5,40},{6,72},{7,104},{8,16},{9,4... | collective-permute-start | bytes 294920 | tf_op jit(solution)/shard_map/ppermute | solution.py:121
  479.4 15.0 %collective-permute-start.1 = (bf16[128,384]{1,0:T(8,128)(2,1)}, bf16[128,384]{1,0:T(8,128)(2,1)}, u32[]{:S(2)}, u32[]{:S(2)}) collective-permute-start(bf16[128,384]{1,0:T(8,128)(2,1)} %get-tuple-element.30), channel_id=1, source_target_pairs={{0,16},{1,48},{2,80},{3,112},{4,24},{5,56},{6,88},{7,120},{8,0},{9... | collective-permute-start | bytes 294920 | tf_op jit(solution)/shard_map/ppermute | solution.py:121
  487.5 8.5 %copy-start.1 = (s32[16]{0:T(128)S(1)}, s32[16]{0:T(128)}, u32[]{:S(2)}) copy-start(s32[16]{0:T(128)} %param.18) | copy-start | bytes 196
Sparse Core Ops, SparseCore 0:
  50.8 24.9 reduce-scatter.3
  78.2 129.8 reduce-scatter.5
  329.8 36.2 all-gather.1
  394.2 77.1 reduce-scatter.7
